TPU v7x, 256 devices: a whole 4x4x8 slice. The times are simulated.
256 devices in a mesh: dp: 8 (over x, z_lo), seq: 32 (over z_hi, y, core).
Axes of the slice: x: 4, y: 4, z: 8 (z_hi: 4, z_lo: 2; z = z_hi * 2 + z_lo), core: 2. Of those that a mesh axis runs over, the one named last changes fastest.
Arguments:
- inputs: float32 [8, 4096, 2048], P('dp', 'seq'), may hold values from -6 to 6
- cotangent: float32 [8, 4096, 2048], P('dp', 'seq'), may hold values from -6 to 6
- block_mix: float32 [128, 128], replicated, may hold values from -0.5 to 0.5
- twist_hi: float32 [2, 2, 2048], replicated, may hold values from -3 to 3
- twist_lo: float32 [2, 2, 2048], replicated, may hold values from -3 to 3
- gain: float32 [2048], replicated, may hold values from 0.5 to 1.5
- gate_up: float32 [128, 2, 16, 256], P('seq'), may hold values from -0.5 to 0.5
- down: float32 [256, 16, 128], P('seq'), may hold values from -0.375 to 0.375
Outputs:
- grad_inputs: float32 [8, 4096, 2048], P('dp', 'seq')
- grad_gate_up: float32 [128, 2, 16, 256], P('seq')
- grad_down: float32 [256, 16, 128], P('seq')
- grad_block_mix: float32 [128, 128], replicated
- grad_twist_hi: float32 [2, 2, 2048], replicated
- grad_twist_lo: float32 [2, 2, 2048], replicated
- grad_gain: float32 [2048], replicated
All inputs are finite; a program needn't handle non-finite values.
Results may differ from a plain program's by a relative error of at most 0.00022.
Values sent between devices are 32-bit elements; how exact they have to be, the bound alone decides.
No kernel may reach another device: no remote copies, remote signals or barrier semaphores. Data moves between devices by JAX's collectives and lax.ppermute only.
A program may use at most 64 MiB of HBM per device.

v0:
```python
import math

import jax
import jax.numpy as jnp
from jax import lax
from jax.sharding import PartitionSpec as P

NB = 16
BLK = 128
DB = 128


HIGH = lax.Precision.HIGHEST
EPS = 1e-05


def from_partner(block, axis, distance):
    count = lax.axis_size(axis)
    route = []
    for low in range(count):
        high = low | 1 << distance
        if high != low and high < count:
            route += [(low, high), (high, low)]
    return lax.ppermute(block, axis, route)


def side_of(bit):
    return lax.axis_index("seq") // (1 << bit) % 2


def forward_section(field, coeff, bit):
    partner = from_partner(field, "seq", bit)
    own = coeff[side_of(bit)]
    return (own[0] * field + own[1] * partner, partner)


def backward_section(grad, field, partner, coeff, bit):
    side = side_of(bit)
    own = coeff[side]
    sent = from_partner(own[1] * grad, "seq", bit)
    back = own[0] * grad + sent
    term = jnp.stack([jnp.sum(grad * field, axis=0), jnp.sum(grad * partner, axis=0)])
    pick = (jnp.arange(2) == side).astype(jnp.float32)
    return (back, pick[:, None, None] * term[None])


def per_device(inputs, cotangent, block_mix, twist_hi, twist_lo, gain, gate_up, down):
    seq_in = inputs[0]
    tokens, width = seq_in.shape
    count = lax.axis_size("seq")
    top_bit = count.bit_length() - 2
    nblocks = tokens // BLK
    xb = seq_in.reshape(nblocks, BLK, width)
    mixed = jnp.einsum("ij,kjd->kid", block_mix, xb, precision=HIGH).reshape(tokens, width)
    first, mixed_peer = forward_section(mixed, twist_hi, top_bit)
    second, first_peer = forward_section(first, twist_lo, 0)
    resid = seq_in + second
    scale = lax.rsqrt(jnp.mean(resid * resid, axis=-1, keepdims=True) + EPS)
    unit = resid * scale
    normed = (unit * gain).reshape(tokens, NB, DB)
    full_gu, full_down = (
        lax.all_gather(gate_up, "seq", axis=0, tiled=True),
        lax.all_gather(down, "seq", axis=0, tiled=True),
    )
    gate_val = jnp.einsum("tnd,dnf->tnf", normed, full_gu[:, 0], precision=HIGH)
    up_val = jnp.einsum("tnd,dnf->tnf", normed, full_gu[:, 1], precision=HIGH)
    sig = jax.nn.sigmoid(gate_val)
    act = gate_val * sig
    hidden = act * up_val
    grad_out = cotangent[0]
    grad_blocks = grad_out.reshape(tokens, NB, DB)
    grad_hidden = jnp.einsum("tnd,fnd->tnf", grad_blocks, full_down, precision=HIGH)
    grad_gate = grad_hidden * up_val * sig * (1.0 + gate_val * (1.0 - sig))
    grad_up = grad_hidden * act
    grad_normed = jnp.einsum("tnf,dnf->tnd", grad_gate, full_gu[:, 0], precision=HIGH)
    grad_normed = grad_normed + jnp.einsum("tnf,dnf->tnd", grad_up, full_gu[:, 1], precision=HIGH)
    grad_normed = grad_normed.reshape(tokens, width)
    cols = normed
    whole_gu = jnp.stack(
        [
            jnp.einsum("tnd,tnf->dnf", cols, grad_gate, precision=HIGH),
            jnp.einsum("tnd,tnf->dnf", cols, grad_up, precision=HIGH),
        ],
        axis=1,
    )
    cols = hidden
    whole_down = jnp.einsum("tnf,tnd->fnd", cols, grad_blocks, precision=HIGH)
    whole_gu, whole_down = lax.psum((whole_gu, whole_down), "dp")
    part_gu, part_down = (
        lax.psum_scatter(whole_gu, "seq", scatter_dimension=0, tiled=True),
        lax.psum_scatter(whole_down, "seq", scatter_dimension=0, tiled=True),
    )
    grad_gain_local = jnp.sum(grad_normed * unit, axis=0)
    weighted = grad_normed * gain
    inner = jnp.mean(weighted * resid, axis=-1, keepdims=True)
    grad_resid = grad_out + scale * weighted - resid * scale * scale * scale * inner
    grad_first, term_lo = backward_section(grad_resid, first, first_peer, twist_lo, 0)
    grad_mixed, term_hi = backward_section(grad_first, mixed, mixed_peer, twist_hi, top_bit)
    grad_mb = grad_mixed.reshape(nblocks, BLK, width)
    term_block = jnp.einsum("kid,kjd->ij", grad_mb, xb, precision=HIGH)
    grad_seq = jnp.einsum("ij,kid->kjd", block_mix, grad_mb, precision=HIGH).reshape(tokens, width)
    grad_seq = grad_seq + grad_resid
    sum_block, sum_hi, sum_lo, sum_gain = lax.psum(
        (term_block, term_hi, term_lo, grad_gain_local), ("dp", "seq")
    )
    factor = 1.0 / math.sqrt(lax.axis_size("dp") * count * tokens)
    return (
        grad_seq[None],
        part_gu * factor,
        part_down * factor,
        sum_block * factor,
        sum_hi * factor,
        sum_lo * factor,
        sum_gain * factor,
    )


def solution(mesh):
    return jax.shard_map(
        per_device,
        mesh=mesh,
        in_specs=(
            P("dp", "seq", None),
            P("dp", "seq", None),
            P(),
            P(),
            P(),
            P(),
            P("seq", None, None, None),
            P("seq", None, None),
        ),
        out_specs=(
            P("dp", "seq", None),
            P("seq", None, None, None),
            P("seq", None, None),
            P(),
            P(),
            P(),
            P(),
        ),
        check_vma=False,
    )
```

profile of v0, /device:TPU:1, one launch (start us, length us, event | category | flops | bytes accessed | tf_op | source)
XLA Modules:
  0.0 965.4 jit_solution(13173433841976585971)
XLA Ops:
  7.2 1.5 copy.34
  8.8 0.7 all-gather.5.cloned.1.call-update
  9.6 3.0 convolution_bitcast_fusion.1
  12.6 7.8 collective-permute-start
  20.5 28.3 %collective-permute-done = f32[128,2048]{0,1:T(8,128)S(1)} collective-permute-done((f32[128,2048]{0,1:T(8,128)S(1)}, f32[128,2048]{0,1:T(8,128)S(1)}, u32[]{:S(2)}, u32[]{:S(2)}) %collective-permute-start) | collective-permute-done | bytes 1048608 | tf_op jit(solution)/shard_map/ppermute | solution.py:24
  48.8 1.0 copy-done.7
  49.8 1.8 multiply_add_fusion.2
  51.6 18.4 %collective-permute-start.1 = (f32[128,2048]{0,1:T(8,128)S(1)}, f32[128,2048]{0,1:T(8,128)}, u32[]{:S(2)}, u32[]{:S(2)}) collective-permute-start(f32[128,2048]{0,1:T(8,128)S(1)} %multiply_add_fusion.2), channel_id=1, source_target_pairs={{0,1},{1,0},{2,3},{3,2},{4,5},{5,4},{6,7},{7,6},{8,9},{9,8},{10,11... | collective-permute-start | bytes 3145736 | tf_op jit(solution)/shard_map/ppermute | solution.py:24
  70.0 1.3 copy.33
  71.4 2.7 copy.32
  74.3 1.3 copy-done.10
  75.5 2.2 multiply_reduce_fusion.5
  78.1 27.6 %all-gather.3.cloned.1.call-done = f32[256,16,128]{2,0,1:T(8,128)} async-done(((f32[8,16,128]{2,0,1:T(8,128)}), f32[256,16,128]{2,0,1:T(8,128)}) %all-gather.3.cloned.1.call-update) | async-done | bytes 2097168 | tf_op jit(solution)/shard_map/all_gather | solution.py:63
  105.8 5.1 fusion.21
  110.9 55.3 %all-gather.5.cloned.1.call-done = f32[128,2,16,256]{3,2,1,0:T(8,128)} async-done(((f32[4,2,16,256]{3,2,1,0:T(8,128)}), f32[128,2,16,256]{3,2,1,0:T(8,128)}) %all-gather.5.cloned.1.call-update) | async-done | bytes 4194320 | tf_op jit(solution)/shard_map/all_gather | solution.py:62
  166.2 2.7 fusion.26
  168.8 4.6 fusion.12
  173.4 4.5 fusion.10
  178.0 4.1 fusion.9
  182.2 4.1 fusion.14
  186.3 1.3 fusion.18
  187.9 2.2 multiply_reduce_fusion.1
  190.8 0.7 broadcast_multiply_fusion.5
  191.5 1.7 collective-permute-done.2
  193.2 0.9 multiply_reduce_fusion.3
  194.1 0.7 broadcast_multiply_fusion.8
  195.1 6.4 fusion.13
  201.6 4.3 convolution_bitcast_fusion.2
  205.9 2.6 convolution_bitcast_fusion.3
  208.6 2.4 pad_maximum_fusion
  211.0 5.5 copy.46
  216.6 1.3 broadcast_multiply_fusion.1
  217.9 2.0 collective-permute-start.3
  219.9 230.0 %all-reduce.8.cloned.1.call-done = (f32[2,2,2048]{2,1,0:T(2,128)}, f32[2,2,2048]{2,1,0:T(2,128)}, f32[2048]{0:T(1024)}) async-done(((f32[2,2,2048]{2,1,0:T(2,128)}, f32[2,2,2048]{2,1,0:T(2,128)}, f32[2048]{0:T(1024)}), (f32[2,2,2048]{2,1,0:T(2,128)}, f32[2,2,2048]{2,1,0:T(2,128)}, f32[2048]{0:T(1024)})) %all-reduce.8.cloned.1.call-update) | async-done | bytes 73744 | tf_op jit(solution)/shard_map/psum | solution.py:103
  449.9 1.3 broadcast_multiply_fusion.9
  451.2 1.4 broadcast_multiply_fusion.7
  452.6 1.4 broadcast_multiply_fusion.6
  454.0 4.0 fusion.15
  458.1 2.2 fusion.1
  460.3 1.3 copy.48
  461.6 76.4 %reduce-scatter.5.cloned.1.call-done = f32[8,16,128]{2,0,1:T(8,128)} async-done(((f32[256,16,128]{2,0,1:T(8,128)}), f32[8,16,128]{2,0,1:T(8,128)}) %reduce-scatter.5.cloned.1.call-update) | async-done | bytes 65552 | tf_op jit(solution)/shard_map/reduce_scatter | solution.py:91
  538.0 101.2 %reduce-scatter.3.cloned.1.call-done = f32[4,2,16,256]{3,2,1,0:T(8,128)} async-done(((f32[128,2,16,256]{3,2,1,0:T(8,128)}), f32[4,2,16,256]{3,2,1,0:T(8,128)}) %reduce-scatter.3.cloned.1.call-update) | async-done | bytes 131088 | tf_op jit(solution)/shard_map/reduce_scatter | solution.py:90
  639.3 243.9 %all-reduce.6.cloned.1.call-done = f32[128,128]{1,0:T(8,128)} async-done(((f32[128,128]{1,0:T(8,128)}), f32[128,128]{1,0:T(8,128)}) %all-reduce.6.cloned.1.call-update) | async-done | bytes 65552 | tf_op jit(solution)/shard_map/psum | solution.py:103
  883.2 1.5 broadcast_multiply_fusion.3
  884.6 70.6 %all-reduce.10.cloned.1.call-done = (f32[4,2,16,256]{3,2,1,0:T(8,128)}, f32[8,16,128]{2,0,1:T(8,128)}) async-done(((f32[4,2,16,256]{3,2,1,0:T(8,128)}, f32[8,16,128]{2,0,1:T(8,128)}), (f32[4,2,16,256]{3,2,1,0:T(8,128)}, f32[8,16,128]{2,0,1:T(8,128)})) %all-reduce.10.cloned.1.call-update) | async-done | bytes 196624 | tf_op jit(solution)/shard_map/psum | solution.py:88
  955.2 1.6 broadcast_multiply_fusion.2
  956.8 0.8 broadcast_multiply_fusion.4
  957.7 0.6 copy.49
  (68 shorter events, 2.2 us)
Async XLA Ops:
  7.2 2.4 copy-start
  7.2 13.3 %copy-start.20 = (f32[2,2,2048]{2,1,0:T(2,128)S(1)}, f32[2,2,2048]{2,1,0:T(2,128)}, u32[]{:S(2)}) copy-start(f32[2,2,2048]{2,1,0:T(2,128)} %param.12) | copy-start | bytes 98308
  7.2 13.3 %copy-start.21 = (f32[2,2,2048]{2,1,0:T(2,128)S(1)}, f32[2,2,2048]{2,1,0:T(2,128)}, u32[]{:S(2)}) copy-start(f32[2,2,2048]{2,1,0:T(2,128)} %param.11) | copy-start | bytes 98308
  7.2 98.6 %all-gather.3.cloned.1.call-start = ((), (), s32[]{:S(2)}) async-start(), calls=%async_computation.2 | async-start | bytes 2162688 | tf_op jit(solution)/shard_map/all_gather | solution.py:63
  8.8 157.4 %all-gather.5.cloned.1.call-start = ((), (), s32[]{:S(2)}) async-start(), calls=%async_computation.3 | async-start | bytes 4325376 | tf_op jit(solution)/shard_map/all_gather | solution.py:62
  9.5 440.4 %all-reduce.8.cloned.1.call-start = ((), (), s32[]{:S(2)}) async-start(), calls=%async_computation.7 | async-start | bytes 147456 | tf_op jit(solution)/shard_map/psum | solution.py:103
  12.6 58.7 %copy-start.1 = (f32[128,2048]{0,1:T(8,128)}, f32[128,2048]{0,1:T(8,128)S(1)}, u32[]{:S(2)}) copy-start(f32[128,2048]{0,1:T(8,128)S(1)} %convolution_bitcast_fusion.1) | copy-start | bytes 3145732
  12.6 57.4 %copy-start.3 = (f32[1,128,2048]{2,1,0:T(8,128)S(1)}, f32[1,128,2048]{2,1,0:T(8,128)}, u32[]{:S(2)}) copy-start(f32[1,128,2048]{2,1,0:T(8,128)} %param.8) | copy-start | bytes 3145732
  12.6 36.2 %collective-permute-start = (f32[128,2048]{0,1:T(8,128)S(1)}, f32[128,2048]{0,1:T(8,128)S(1)}, u32[]{:S(2)}, u32[]{:S(2)}) collective-permute-start(f32[128,2048]{0,1:T(8,128)S(1)} %convolution_bitcast_fusion.1), channel_id=1, source_target_pairs={{0,16},{16,0},{1,17},{17,1},{2,18},{18,2},{3,19},{19,3},{4,20},{20... | collective-permute-start | bytes 3145736 | tf_op jit(solution)/shard_map/ppermute | solution.py:24
  48.8 1.0 copy-start.7
  51.6 22.6 %copy-start.5 = (f32[128,2048]{0,1:T(8,128)}, f32[128,2048]{0,1:T(8,128)S(1)}, u32[]{:S(2)}) copy-start(f32[128,2048]{0,1:T(8,128)S(1)} %multiply_add_fusion.2) | copy-start | bytes 3145732
  51.6 22.6 %collective-permute-start.1 = (f32[128,2048]{0,1:T(8,128)S(1)}, f32[128,2048]{0,1:T(8,128)}, u32[]{:S(2)}, u32[]{:S(2)}) collective-permute-start(f32[128,2048]{0,1:T(8,128)S(1)} %multiply_add_fusion.2), channel_id=1, source_target_pairs={{0,1},{1,0},{2,3},{3,2},{4,5},{5,4},{6,7},{7,6},{8,9},{9,8},{10,11... | collective-permute-start | bytes 3145736 | tf_op jit(solution)/shard_map/ppermute | solution.py:24
  71.4 2.7 copy-start.11
  74.0 1.5 copy-start.10
  74.2 31.5 %copy-start.9 = (f32[16,8,16,128]{3,2,1,0:T(8,128)}, f32[16,8,16,128]{3,2,1,0:T(8,128)S(1)}, u32[]{:S(2)}) copy-start(f32[16,8,16,128]{3,2,1,0:T(8,128)S(1)} %copy.60) | copy-start | bytes 3145732
  75.5 2.3 copy-start.19
  173.4 8.7 copy-start.15
  173.4 4.6 copy-start.13
  178.0 4.2 copy-start.17
  186.3 1.3 copy-start.6
  186.3 1.5 copy-start.12
  190.1 3.1 copy-start.2
  190.1 3.1 copy-start.8
  190.4 2.7 collective-permute-start.2
  194.9 343.2 %reduce-scatter.5.cloned.1.call-start = ((), (), s32[]{:S(2)}) async-start(), calls=%async_computation.6 | async-start | bytes 2162688 | tf_op jit(solution)/shard_map/reduce_scatter | solution.py:91
  201.5 437.7 %reduce-scatter.3.cloned.1.call-start = ((), (), s32[]{:S(2)}) async-start(), calls=%async_computation.5 | async-start | bytes 4325376 | tf_op jit(solution)/shard_map/reduce_scatter | solution.py:90
  201.6 4.3 copy-start.14
  201.6 4.3 copy-start.16
  201.6 4.3 copy-start.18
  216.5 237.5 %copy-start.4 = (f32[1,128,2048]{2,1,0:T(8,128)S(1)}, f32[1,128,2048]{2,1,0:T(8,128)}, u32[]{:S(2)}) copy-start(f32[1,128,2048]{2,1,0:T(8,128)} %param.8) | copy-start | bytes 3145732
  216.5 666.6 %all-reduce.6.cloned.1.call-start = ((), (), s32[]{:S(2)}) async-start(), calls=%async_computation.4 | async-start | bytes 131072 | tf_op jit(solution)/shard_map/psum | solution.py:103
  217.9 236.1 %collective-permute-start.3 = (f32[128,2048]{0,1:T(8,128)}, f32[128,2048]{0,1:T(8,128)}, u32[]{:S(2)}, u32[]{:S(2)}) collective-permute-start(f32[128,2048]{0,1:T(8,128)} %broadcast_multiply_fusion.1), channel_id=1, source_target_pairs={{0,16},{16,0},{1,17},{17,1},{2,18},{18,2},{3,19},{19,3},{4,20},{20... | collective-permute-start | bytes 3145736 | tf_op jit(solution)/shard_map/ppermute | solution.py:24
  458.0 497.2 %all-reduce.10.cloned.1.call-start = ((), (), s32[]{:S(2)}) async-start(), calls=%async_computation.8 | async-start | bytes 393216 | tf_op jit(solution)/shard_map/psum | solution.py:88
Sparse Core Ops, SparseCore 0:
  11.1 94.6 all-gather.2
  108.3 57.7 all-gather.4
  195.0 254.8 all-reduce.7
  453.6 84.3 reduce-scatter.4
  541.8 97.3 reduce-scatter.2
  646.1 237.0 all-reduce.5
  886.0 69.1 all-reduce.9
where the time goes:
time: 974 us; the launch traced here: 965 us
  waiting for transfers between devices  836 us (86%)
  matrix products  45.1 us (5%)
  starting transfers between devices  29.1 us (3%)
  other arithmetic  22.3 us (2%)
  local copies, waits for them, and re-layouts  18.4 us (2%)
  between operations  14.7 us (2%)
    psum x2, waiting for transfers between devices, per_device(): lax.psum((term_block, term_hi, term_lo, grad_gain_local), ('dp', 'seq'))  474 us
    reduce_scatter x1, waiting for transfers between devices, per_device(): lax.psum_scatter(whole_gu, 'seq', scatter_dimension=0, tiled=True)  101 us
    reduce_scatter x1, waiting for transfers between devices, per_device(): lax.psum_scatter(whole_down, 'seq', scatter_dimension=0, tiled=True)  76.4 us
    psum x1, waiting for transfers between devices, per_device(): whole_gu, whole_down = lax.psum((whole_gu, whole_down), 'dp')  70.6 us
    all_gather x1, waiting for transfers between devices, per_device(): lax.all_gather(gate_up, 'seq', axis=0, tiled=True)  55.3 us
    ppermute x4, waiting for transfers between devices, from_partner(): return lax.ppermute(block, axis, route)  30 us
    ppermute x4, starting transfers between devices, from_partner(): return lax.ppermute(block, axis, route)  28.6 us
    all_gather x1, waiting for transfers between devices, per_device(): lax.all_gather(down, 'seq', axis=0, tiled=True)  27.6 us
  transfers between devices with their start and end apart: 11, of which 9 were waited for; matrix products, arithmetic and copies ran while one was open for 6% of the time, Pallas kernels for 0%

commit v1 on v0

--- a/solution.py
+++ b/solution.py
@@ -44,12 +44,47 @@
     return (back, pick[:, None, None] * term[None])
 
 
+def exchange(x):
+    return lax.all_to_all(x, "seq", 0, 0, tiled=True)
+
+
+def to_blocks(field, count):
+    tokens = field.shape[0]
+    halves = count // NB
+    x = field.reshape(halves, tokens // halves, NB, DB)
+    x = jnp.transpose(x, (2, 0, 1, 3))
+    return x.reshape(count, tokens // halves, DB)
+
+
+def from_blocks(x, tokens, count):
+    halves = count // NB
+    x = x.reshape(NB, halves, tokens // halves, DB)
+    x = jnp.transpose(x, (1, 2, 0, 3))
+    return x.reshape(tokens, NB * DB)
+
+
 def per_device(inputs, cotangent, block_mix, twist_hi, twist_lo, gain, gate_up, down):
     seq_in = inputs[0]
     tokens, width = seq_in.shape
     count = lax.axis_size("seq")
+    halves = count // NB
     top_bit = count.bit_length() - 2
     nblocks = tokens // BLK
+    rows_gu = gate_up.shape[0]
+    rows_dn = down.shape[0]
+    fb = gate_up.shape[3]
+
+    gu_n = jnp.transpose(gate_up, (2, 0, 1, 3)).reshape(NB, rows_gu * 2 * fb)
+    dn_n = jnp.transpose(down, (1, 0, 2)).reshape(NB, rows_dn * DB)
+    wbuf = jnp.concatenate([gu_n, dn_n], axis=1)
+    wbuf = jnp.repeat(wbuf, halves, axis=0)
+    wrecv = exchange(wbuf)
+    w_gu = wrecv[:, : rows_gu * 2 * fb].reshape(count * rows_gu, 2, fb)
+    w_dn = wrecv[:, rows_gu * 2 * fb :].reshape(count * rows_dn, DB)
+
+    grad_out = cotangent[0]
+    cot_blk = exchange(to_blocks(grad_out, count)).reshape(-1, DB)
+
     xb = seq_in.reshape(nblocks, BLK, width)
     mixed = jnp.einsum("ij,kjd->kid", block_mix, xb, precision=HIGH).reshape(tokens, width)
     first, mixed_peer = forward_section(mixed, twist_hi, top_bit)
@@ -57,39 +92,30 @@
     resid = seq_in + second
     scale = lax.rsqrt(jnp.mean(resid * resid, axis=-1, keepdims=True) + EPS)
     unit = resid * scale
-    normed = (unit * gain).reshape(tokens, NB, DB)
-    full_gu, full_down = (
-        lax.all_gather(gate_up, "seq", axis=0, tiled=True),
-        lax.all_gather(down, "seq", axis=0, tiled=True),
-    )
-    gate_val = jnp.einsum("tnd,dnf->tnf", normed, full_gu[:, 0], precision=HIGH)
-    up_val = jnp.einsum("tnd,dnf->tnf", normed, full_gu[:, 1], precision=HIGH)
+    normed = unit * gain
+    x_blk = exchange(to_blocks(normed, count)).reshape(-1, DB)
+
+    gate_val = jnp.dot(x_blk, w_gu[:, 0], precision=HIGH)
+    up_val = jnp.dot(x_blk, w_gu[:, 1], precision=HIGH)
     sig = jax.nn.sigmoid(gate_val)
     act = gate_val * sig
     hidden = act * up_val
-    grad_out = cotangent[0]
-    grad_blocks = grad_out.reshape(tokens, NB, DB)
-    grad_hidden = jnp.einsum("tnd,fnd->tnf", grad_blocks, full_down, precision=HIGH)
+    grad_hidden = jnp.dot(cot_blk, w_dn.T, precision=HIGH)
     grad_gate = grad_hidden * up_val * sig * (1.0 + gate_val * (1.0 - sig))
     grad_up = grad_hidden * act
-    grad_normed = jnp.einsum("tnf,dnf->tnd", grad_gate, full_gu[:, 0], precision=HIGH)
-    grad_normed = grad_normed + jnp.einsum("tnf,dnf->tnd", grad_up, full_gu[:, 1], precision=HIGH)
-    grad_normed = grad_normed.reshape(tokens, width)
-    cols = normed
-    whole_gu = jnp.stack(
-        [
-            jnp.einsum("tnd,tnf->dnf", cols, grad_gate, precision=HIGH),
-            jnp.einsum("tnd,tnf->dnf", cols, grad_up, precision=HIGH),
-        ],
-        axis=1,
-    )
-    cols = hidden
-    whole_down = jnp.einsum("tnf,tnd->fnd", cols, grad_blocks, precision=HIGH)
-    whole_gu, whole_down = lax.psum((whole_gu, whole_down), "dp")
-    part_gu, part_down = (
-        lax.psum_scatter(whole_gu, "seq", scatter_dimension=0, tiled=True),
-        lax.psum_scatter(whole_down, "seq", scatter_dimension=0, tiled=True),
-    )
+    grad_x = jnp.dot(grad_gate, w_gu[:, 0].T, precision=HIGH) + jnp.dot(grad_up, w_gu[:, 1].T, precision=HIGH)
+    grad_normed = from_blocks(exchange(grad_x.reshape(count, -1, DB)), tokens, count)
+
+    d_gate = jnp.dot(x_blk.T, grad_gate, precision=HIGH)
+    d_up = jnp.dot(x_blk.T, grad_up, precision=HIGH)
+    d_gu = jnp.stack([d_gate, d_up], axis=1).reshape(count, rows_gu * 2 * fb)
+    d_dn = jnp.dot(hidden.T, cot_blk, precision=HIGH).reshape(count, rows_dn * DB)
+    grecv = exchange(jnp.concatenate([d_gu, d_dn], axis=1))
+    grecv = grecv.reshape(NB, halves, -1).sum(axis=1)
+    part_gu = jnp.transpose(grecv[:, : rows_gu * 2 * fb].reshape(NB, rows_gu, 2, fb), (1, 2, 0, 3))
+    part_down = jnp.transpose(grecv[:, rows_gu * 2 * fb :].reshape(NB, rows_dn, DB), (1, 0, 2))
+    part_gu, part_down = lax.psum((part_gu, part_down), "dp")
+
     grad_gain_local = jnp.sum(grad_normed * unit, axis=0)
     weighted = grad_normed * gain
     inner = jnp.mean(weighted * resid, axis=-1, keepdims=True)

time: 974 us -> 794 us (0.82)
  waiting for transfers between devices: 836 us -> 631 us
  starting transfers between devices: 29.1 us -> 52.5 us
    reduce_scatter x2 -> x0, waiting for transfers between devices: 178 us -> none  [the longest x1 101 us: per_device(): lax.psum_scatter(whole_gu, 'seq', scatter_dimension=0, tiled=True)]
    all_to_all x0 -> x5, waiting for transfers between devices: none -> 97.3 us  [exchange(): return lax.all_to_all(x, 'seq', 0, 0, tiled=True)]
    all_gather x2 -> x0, waiting for transfers between devices: 82.9 us -> none  [the longest x1 55.3 us: per_device(): lax.all_gather(gate_up, 'seq', axis=0, tiled=True)]
    all_to_all x0 -> x5, starting transfers between devices: none -> 38.3 us  [exchange(): return lax.all_to_all(x, 'seq', 0, 0, tiled=True)]
    ppermute x4, waiting for transfers between devices: 30 us -> 2.36 us  [from_partner(): return lax.ppermute(block, axis, route)]
    ppermute x4, starting transfers between devices: 28.6 us -> 13.8 us  [from_partner(): return lax.ppermute(block, axis, route)]
    psum x1, waiting for transfers between devices: 70.6 us -> 55.9 us  [per_device(): part_gu, part_down = lax.psum((part_gu, part_down), 'dp')]
  transfers between devices with their start and end apart: 11 -> 12, of which waited for: 9 -> 9; matrix products, arithmetic and copies ran while one was open for 6% -> 6% of each run, Pallas kernels for 0% -> 0%
where the time goes in v1:
time: 794 us; the launch traced here: 787 us
  waiting for transfers between devices  631 us (79%)
  starting transfers between devices  52.5 us (7%)
  matrix products  42 us (5%)
  local copies, waits for them, and re-layouts  23.6 us (3%)
  other arithmetic  21.3 us (3%)
  between operations  16.5 us (2%)
    psum x2, waiting for transfers between devices, per_device(): lax.psum((term_block, term_hi, term_lo, grad_gain_local), ('dp', 'seq'))  476 us
    all_to_all x5, waiting for transfers between devices, exchange(): return lax.all_to_all(x, 'seq', 0, 0, tiled=True)  97.3 us
    psum x1, waiting for transfers between devices, per_device(): part_gu, part_down = lax.psum((part_gu, part_down), 'dp')  55.9 us
    all_to_all x5, starting transfers between devices, exchange(): return lax.all_to_all(x, 'seq', 0, 0, tiled=True)  38.3 us
  transfers between devices with their start and end apart: 12, of which 9 were waited for; matrix products, arithmetic and copies ran while one was open for 6% of the time, Pallas kernels for 0%

profile of v1, /device:TPU:1, one launch (start us, length us, event | category | flops | bytes accessed | tf_op | source)
XLA Modules:
  0.0 787.3 jit_solution(7601056932142582993)
XLA Ops:
  8.8 2.3 convolution_bitcast_fusion.2
  11.2 7.8 collective-permute-start
  20.1 2.4 all_to_all.23
  22.5 6.5 all-to-all-start
  29.4 1.3 copy.50
  30.8 45.8 %all-to-all-done = f32[32,1,3072]{2,1,0:T(1,128)} async-done(((f32[32,1,3072]{2,1,0:T(1,128)}), f32[32,1,3072]{2,1,0:T(1,128)}, u32[]{:S(2)}, u32[]{:S(2)}) %all-to-all-start) | async-done | bytes 393248 | tf_op jit(solution)/shard_map/all_to_all | solution.py:48
  76.6 6.7 all-to-all-start.1
  83.9 2.4 collective-permute-done.1
  87.8 1.3 copy.51
  89.1 18.3 %all-to-all-done.1 = f32[32,64,128]{2,1,0:T(8,128)} async-done(((f32[32,64,128]{2,1,0:T(8,128)}), f32[32,64,128]{2,1,0:T(8,128)}, u32[]{:S(2)}, u32[]{:S(2)}) %all-to-all-start.1) | async-done | bytes 1048608 | tf_op jit(solution)/shard_map/all_to_all | solution.py:48
  107.4 10.0 %all-to-all-start.2 = ((f32[32,64,128]{2,1,0:T(8,128)}), f32[32,64,128]{2,1,0:T(8,128)S(1)}, u32[]{:S(2)}, u32[]{:S(2)}) async-start(f32[32,64,128]{2,1,0:T(8,128)} %bitcast.126), calls=%async_computation.2 | async-start | bytes 2097152 | tf_op jit(solution)/shard_map/all_to_all | solution.py:48
  117.4 1.1 copy.99
  119.9 1.2 reshape.129
  121.0 1.6 reshape.123
  123.5 4.5 convolution_bitcast_fusion
  128.0 13.7 %all-to-all-done.2 = f32[32,64,128]{2,1,0:T(8,128)S(1)} async-done(((f32[32,64,128]{2,1,0:T(8,128)}), f32[32,64,128]{2,1,0:T(8,128)S(1)}, u32[]{:S(2)}, u32[]{:S(2)}) %all-to-all-start.2) | async-done | bytes 1048608 | tf_op jit(solution)/shard_map/all_to_all | solution.py:48
  141.7 1.8 fusion.17
  143.6 4.0 add_multiply_fusion
  147.5 4.8 fusion.2
  152.4 3.2 convolution_bitcast_fusion.3
  155.5 1.6 reshape.135
  157.1 3.7 convolution_bitcast_fusion.4
  161.3 0.9 maximum_bitcast_fusion
  162.2 1.2 copy.60
  163.4 9.5 %all-to-all-start.4 = ((f32[32,1,3072]{2,1,0:T(1,128)}), f32[32,1,3072]{2,1,0:T(1,128)S(1)}, u32[]{:S(2)}, u32[]{:S(2)}) async-start(f32[32,1,3072]{2,1,0:T(1,128)} %copy.60), calls=%async_computation.4 | async-start | bytes 786432 | tf_op jit(solution)/shard_map/all_to_all | solution.py:48
  172.9 5.2 fusion.12
  178.1 6.2 convolution_add_fusion
  184.4 4.2 all-to-all-done.4
  189.3 5.6 all-to-all-start.3
  196.0 2.7 reduce
  198.7 2.0 reshape.136
  200.7 1.5 reduce_sum.74
  203.9 15.4 %all-to-all-done.3 = f32[32,64,128]{2,1,0:T(8,128)S(1)} async-done(((f32[32,64,128]{2,1,0:T(8,128)}), f32[32,64,128]{2,1,0:T(8,128)S(1)}, u32[]{:S(2)}, u32[]{:S(2)}) %all-to-all-start.3) | async-done | bytes 1048608 | tf_op jit(solution)/shard_map/all_to_all | solution.py:48
  219.9 1.3 fusion.5
  222.3 0.9 collective-permute-start.2
  223.2 55.9 %all-reduce.10.cloned.1.call-done = (f32[4,2,16,256]{3,1,0,2:T(2,128)}, f32[8,16,128]{2,0,1:T(8,128)}) async-done(((f32[4,2,16,256]{3,1,0,2:T(2,128)}, f32[8,16,128]{2,0,1:T(8,128)}), (f32[4,2,16,256]{3,1,0,2:T(2,128)}, f32[8,16,128]{2,0,1:T(8,128)})) %all-reduce.10.cloned.1.call-update) | async-done | bytes 196624 | tf_op jit(solution)/shard_map/psum | solution.py:117
  279.1 1.0 broadcast_multiply_fusion.2
  283.0 2.3 multiply_reduce_fusion.3
  286.1 1.1 broadcast_multiply_fusion.1
  287.2 4.6 collective-permute-start.3
  291.8 246.4 %all-reduce.8.cloned.1.call-done = (f32[2,2,2048]{2,1,0:T(2,128)}, f32[2,2,2048]{2,1,0:T(2,128)}, f32[2048]{0:T(1024)}) async-done(((f32[2,2,2048]{2,1,0:T(2,128)}, f32[2,2,2048]{2,1,0:T(2,128)}, f32[2048]{0:T(1024)}), (f32[2,2,2048]{2,1,0:T(2,128)}, f32[2,2,2048]{2,1,0:T(2,128)}, f32[2048]{0:T(1024)})) %all-reduce.8.cloned.1.call-update) | async-done | bytes 73744 | tf_op jit(solution)/shard_map/psum | solution.py:129
  538.2 1.3 broadcast_multiply_fusion.9
  539.5 1.4 broadcast_multiply_fusion.7
  540.9 1.4 broadcast_multiply_fusion.6
  542.3 2.9 fusion.6
  545.2 3.3 fusion.1
  548.6 229.4 %all-reduce.6.cloned.1.call-done = f32[128,128]{1,0:T(8,128)} async-done(((f32[128,128]{1,0:T(8,128)}), f32[128,128]{1,0:T(8,128)}) %all-reduce.6.cloned.1.call-update) | async-done | bytes 65552 | tf_op jit(solution)/shard_map/psum | solution.py:129
  778.0 1.5 broadcast_multiply_fusion.3
  (110 shorter events, 16.0 us)
Async XLA Ops:
  8.0 0.8 copy-start
  8.0 11.0 %copy-start.24 = (f32[8,16,128]{2,1,0:T(8,128)S(1)}, f32[8,16,128]{2,1,0:T(8,128)}, u32[]{:S(2)}) copy-start(f32[8,16,128]{2,1,0:T(8,128)} %param.15) | copy-start | bytes 196612
  8.0 11.0 %copy-start.15 = (f32[4,2,16,256]{3,2,1,0:T(8,128)S(1)}, f32[4,2,16,256]{3,2,1,0:T(8,128)}, u32[]{:S(2)}) copy-start(f32[4,2,16,256]{3,2,1,0:T(8,128)} %param.14) | copy-start | bytes 393220
  11.1 72.2 %copy-start.2 = (f32[128,2048]{1,0:T(8,128)}, f32[128,2048]{1,0:T(8,128)S(1)}, u32[]{:S(2)}) copy-start(f32[128,2048]{1,0:T(8,128)S(1)} %convolution_bitcast_fusion.2) | copy-start | bytes 3145732
  11.1 17.9 %copy-start.8 = (f32[1,128,2048]{2,1,0:T(8,128)S(1)}, f32[1,128,2048]{2,1,0:T(8,128)}, u32[]{:S(2)}) copy-start(f32[1,128,2048]{2,1,0:T(8,128)} %param.9) | copy-start | bytes 3145732
  11.2 72.1 %collective-permute-start = (f32[128,2048]{1,0:T(8,128)S(1)}, f32[128,2048]{1,0:T(8,128)S(1)}, u32[]{:S(2)}, u32[]{:S(2)}) collective-permute-start(f32[128,2048]{1,0:T(8,128)S(1)} %convolution_bitcast_fusion.2), channel_id=1, source_target_pairs={{0,16},{16,0},{1,17},{17,1},{2,18},{18,2},{3,19},{19,3},{4,20},{20... | collective-permute-start | bytes 3145736 | tf_op jit(solution)/shard_map/ppermute | solution.py:24
  22.5 54.1 %all-to-all-start = ((f32[32,1,3072]{2,1,0:T(1,128)}), f32[32,1,3072]{2,1,0:T(1,128)}, u32[]{:S(2)}, u32[]{:S(2)}) async-start(f32[32,1,3072]{2,1,0:T(1,128)} %all_to_all.23), calls=%async_computation | async-start | bytes 786432 | tf_op jit(solution)/shard_map/all_to_all | solution.py:48
  29.3 1.4 copy-start.25
  29.3 1.4 copy-start.26
  30.7 52.7 %copy-start.18 = (f32[1,1,2048]{2,1,0:T(1,128)}, f32[1,1,2048]{2,1,0:T(1,128)S(1)}, u32[]{:S(2)}) copy-start(f32[1,1,2048]{2,1,0:T(1,128)S(1)} %get-tuple-element.51) | copy-start | bytes 24580
  30.8 55.5 %copy-start.20 = (f32[1,1,2048]{2,1,0:T(1,128)}, f32[1,1,2048]{2,1,0:T(1,128)S(1)}, u32[]{:S(2)}) copy-start(f32[1,1,2048]{2,1,0:T(1,128)S(1)} %get-tuple-element.45) | copy-start | bytes 24580
  30.8 55.5 %copy-start.22 = (f32[1,1,2048]{2,1,0:T(1,128)}, f32[1,1,2048]{2,1,0:T(1,128)S(1)}, u32[]{:S(2)}) copy-start(f32[1,1,2048]{2,1,0:T(1,128)S(1)} %get-tuple-element.46) | copy-start | bytes 24580
  76.6 30.8 %all-to-all-start.1 = ((f32[32,64,128]{2,1,0:T(8,128)}), f32[32,64,128]{2,1,0:T(8,128)}, u32[]{:S(2)}, u32[]{:S(2)}) async-start(f32[32,64,128]{2,1,0:T(8,128)} %bitcast.14), calls=%async_computation.1 | async-start | bytes 2097152 | tf_op jit(solution)/shard_map/all_to_all | solution.py:48
  83.3 3.0 copy-start.1
  83.3 3.4 copy-start.5
  83.5 3.2 copy-start.3
  83.5 2.7 collective-permute-start.1
  86.2 1.0 copy-start.6
  86.3 1.0 copy-start.17
  87.3 0.5 copy-start.27
  107.4 34.3 %all-to-all-start.2 = ((f32[32,64,128]{2,1,0:T(8,128)}), f32[32,64,128]{2,1,0:T(8,128)S(1)}, u32[]{:S(2)}, u32[]{:S(2)}) async-start(f32[32,64,128]{2,1,0:T(8,128)} %bitcast.126), calls=%async_computation.2 | async-start | bytes 2097152 | tf_op jit(solution)/shard_map/all_to_all | solution.py:48
  123.5 18.2 %copy-start.13 = (f32[128,1,256]{2,1,0:T(1,128)S(1)}, f32[128,1,256]{2,1,0:T(1,128)}, u32[]{:S(2)}) copy-start(f32[128,1,256]{2,1,0:T(1,128)} %get-tuple-element.43) | copy-start | bytes 393220
  128.0 15.5 %copy-start.14 = (f32[128,1,256]{2,1,0:T(1,128)S(1)}, f32[128,1,256]{2,1,0:T(1,128)}, u32[]{:S(2)}) copy-start(f32[128,1,256]{2,1,0:T(1,128)} %get-tuple-element.44) | copy-start | bytes 393220
  141.7 1.9 copy-start.10
  147.5 4.9 copy-start.31
  157.1 3.7 copy-start.16
  163.4 25.2 %all-to-all-start.4 = ((f32[32,1,3072]{2,1,0:T(1,128)}), f32[32,1,3072]{2,1,0:T(1,128)S(1)}, u32[]{:S(2)}, u32[]{:S(2)}) async-start(f32[32,1,3072]{2,1,0:T(1,128)} %copy.60), calls=%async_computation.4 | async-start | bytes 786432 | tf_op jit(solution)/shard_map/all_to_all | solution.py:48
  172.9 5.3 copy-start.11
  188.6 0.7 copy-start.12
  189.3 30.0 %all-to-all-start.3 = ((f32[32,64,128]{2,1,0:T(8,128)}), f32[32,64,128]{2,1,0:T(8,128)S(1)}, u32[]{:S(2)}, u32[]{:S(2)}) async-start(f32[32,64,128]{2,1,0:T(8,128)} %bitcast.132), calls=%async_computation.3 | async-start | bytes 2097152 | tf_op jit(solution)/shard_map/all_to_all | solution.py:48
  194.9 84.2 %all-reduce.10.cloned.1.call-start = ((), (), s32[]{:S(2)}) async-start(), calls=%async_computation.7 | async-start | bytes 393216 | tf_op jit(solution)/shard_map/psum | solution.py:117
  202.9 17.0 %copy-start.28 = (f32[128]{0:T(128)S(1)}, f32[128]{0:T(128)}, u32[]{:S(2)}) copy-start(f32[128]{0:T(128)} %copy-done.27) | copy-start | bytes 1540
  203.6 334.6 %all-reduce.8.cloned.1.call-start = ((), (), s32[]{:S(2)}) async-start(), calls=%async_computation.6 | async-start | bytes 147456 | tf_op jit(solution)/shard_map/psum | solution.py:129
  219.3 1.9 copy-start.4
  219.3 1.9 copy-start.7
  219.3 1.9 copy-start.9
  221.2 0.9 copy-start.23
  222.1 60.2 %copy-start.30 = (f32[2]{0:T(128)S(1)}, f32[2]{0:T(128)}, u32[]{:S(2)}) copy-start(f32[2]{0:T(128)} %compare_convert_fusion) | copy-start | bytes 28
  222.1 60.9 %copy-start.21 = (f32[1,1,2048]{2,1,0:T(1,128)S(1)}, f32[1,1,2048]{2,1,0:T(1,128)}, u32[]{:S(2)}) copy-start(f32[1,1,2048]{2,1,0:T(1,128)} %copy-done.20) | copy-start | bytes 24580
  222.3 60.8 %collective-permute-start.2 = (f32[128,2048]{1,0:T(8,128)S(1)}, f32[128,2048]{1,0:T(8,128)}, u32[]{:S(2)}, u32[]{:S(2)}) collective-permute-start(f32[128,2048]{1,0:T(8,128)S(1)} %broadcast_multiply_fusion), channel_id=1, source_target_pairs={{0,1},{1,0},{2,3},{3,2},{4,5},{5,4},{6,7},{7,6},{8,9},{9,8},{10,11... | collective-permute-start | bytes 3145736 | tf_op jit(solution)/shard_map/ppermute | solution.py:24
  283.0 2.3 copy-start.29
  283.0 3.1 copy-start.19
  286.0 491.9 %all-reduce.6.cloned.1.call-start = ((), (), s32[]{:S(2)}) async-start(), calls=%async_computation.5 | async-start | bytes 131072 | tf_op jit(solution)/shard_map/psum | solution.py:129
  287.2 255.1 %collective-permute-start.3 = (f32[128,2048]{1,0:T(8,128)}, f32[128,2048]{1,0:T(8,128)}, u32[]{:S(2)}, u32[]{:S(2)}) collective-permute-start(f32[128,2048]{1,0:T(8,128)} %broadcast_multiply_fusion.1), channel_id=1, source_target_pairs={{0,16},{16,0},{1,17},{17,1},{2,18},{18,2},{3,19},{19,3},{4,20},{20... | collective-permute-start | bytes 3145736 | tf_op jit(solution)/shard_map/ppermute | solution.py:24
Sparse Core Ops, SparseCore 0:
  203.7 75.3 all-reduce.9
Sparse Core Ops, SparseCore 1:
  286.1 252.0 all-reduce.7
  545.3 232.6 all-reduce.5

commit v2 on v1

--- a/solution.py
+++ b/solution.py
@@ -42,6 +42,12 @@
     term = jnp.stack([jnp.sum(grad * field, axis=0), jnp.sum(grad * partner, axis=0)])
     pick = (jnp.arange(2) == side).astype(jnp.float32)
     return (back, pick[:, None, None] * term[None])
+
+
+def psum_doubling(x, axis):
+    for bit in range(lax.axis_size(axis).bit_length() - 1):
+        x = x + from_partner(x, axis, bit)
+    return x
 
 
 def exchange(x):
@@ -114,7 +120,10 @@
     grecv = grecv.reshape(NB, halves, -1).sum(axis=1)
     part_gu = jnp.transpose(grecv[:, : rows_gu * 2 * fb].reshape(NB, rows_gu, 2, fb), (1, 2, 0, 3))
     part_down = jnp.transpose(grecv[:, rows_gu * 2 * fb :].reshape(NB, rows_dn, DB), (1, 0, 2))
-    part_gu, part_down = lax.psum((part_gu, part_down), "dp")
+    n_gu = part_gu.size
+    wsum = psum_doubling(jnp.concatenate([part_gu.reshape(-1), part_down.reshape(-1)]), "dp")
+    part_gu = wsum[:n_gu].reshape(part_gu.shape)
+    part_down = wsum[n_gu:].reshape(part_down.shape)
 
     grad_gain_local = jnp.sum(grad_normed * unit, axis=0)
     weighted = grad_normed * gain
@@ -126,9 +135,17 @@
     term_block = jnp.einsum("kid,kjd->ij", grad_mb, xb, precision=HIGH)
     grad_seq = jnp.einsum("ij,kid->kjd", block_mix, grad_mb, precision=HIGH).reshape(tokens, width)
     grad_seq = grad_seq + grad_resid
-    sum_block, sum_hi, sum_lo, sum_gain = lax.psum(
-        (term_block, term_hi, term_lo, grad_gain_local), ("dp", "seq")
-    )
+    smalls = (term_block, term_hi, term_lo, grad_gain_local)
+    sbuf = jnp.concatenate([t.reshape(-1) for t in smalls])
+    spart = exchange(sbuf.reshape(count, -1)).sum(axis=0)
+    spart = psum_doubling(spart, "dp")
+    sfull = exchange(jnp.broadcast_to(spart[None], (count, spart.shape[0]))).reshape(-1)
+    sums = []
+    at = 0
+    for t in smalls:
+        sums.append(sfull[at : at + t.size].reshape(t.shape))
+        at += t.size
+    sum_block, sum_hi, sum_lo, sum_gain = sums
     factor = 1.0 / math.sqrt(lax.axis_size("dp") * count * tokens)
     return (
         grad_seq[None],

time: 794 us -> 321 us (0.40)
  waiting for transfers between devices: 631 us -> 157 us
  starting transfers between devices: 52.5 us -> 83 us
  between operations: 16.5 us -> 1.8 us
    psum x3 -> x0, waiting for transfers between devices: 532 us -> none  [the longest x2 476 us: per_device(): lax.psum((term_block, term_hi, term_lo, grad_gain_local), ('dp', 'seq'))]
    ppermute x4 -> x10, waiting for transfers between devices: 2.36 us -> 46 us  [from_partner(): return lax.ppermute(block, axis, route)]
    all_to_all x5 -> x7, starting transfers between devices: 38.3 us -> 62.9 us  [exchange(): return lax.all_to_all(x, 'seq', 0, 0, tiled=True)]
    all_to_all x5 -> x7, waiting for transfers between devices: 97.3 us -> 111 us  [exchange(): return lax.all_to_all(x, 'seq', 0, 0, tiled=True)]
    ppermute x4 -> x10, starting transfers between devices: 13.8 us -> 20.2 us  [from_partner(): return lax.ppermute(block, axis, route)]
  transfers between devices with their start and end apart: 12 -> 17, of which waited for: 9 -> 13; matrix products, arithmetic and copies ran while one was open for 6% -> 16% of each run, Pallas kernels for 0% -> 0%
where the time goes in v2:
time: 321 us; the launch traced here: 315 us
  waiting for transfers between devices  157 us (49%)
  starting transfers between devices  83 us (26%)
  matrix products  35.8 us (11%)
  local copies, waits for them, and re-layouts  22.9 us (7%)
  other arithmetic  14.1 us (4%)
    all_to_all x7, waiting for transfers between devices, exchange(): return lax.all_to_all(x, 'seq', 0, 0, tiled=True)  111 us
    all_to_all x7, starting transfers between devices, exchange(): return lax.all_to_all(x, 'seq', 0, 0, tiled=True)  62.9 us
    ppermute x10, waiting for transfers between devices, from_partner(): return lax.ppermute(block, axis, route)  46 us
    ppermute x10, starting transfers between devices, from_partner(): return lax.ppermute(block, axis, route)  20.2 us
  transfers between devices with their start and end apart: 17, of which 13 were waited for; matrix products, arithmetic and copies ran while one was open for 16% of the time, Pallas kernels for 0%

profile of v2, /device:TPU:1, one launch (start us, length us, event | category | flops | bytes accessed | tf_op | source)
XLA Modules:
  0.0 314.9 jit_solution(12763606251269396324)
XLA Ops:
  1.5 2.3 convolution_bitcast_fusion.2
  3.8 7.8 %collective-permute-start = (f32[128,2048]{1,0:T(8,128)S(1)}, f32[128,2048]{1,0:T(8,128)S(1)}, u32[]{:S(2)}, u32[]{:S(2)}) collective-permute-start(f32[128,2048]{1,0:T(8,128)S(1)} %convolution_bitcast_fusion.2), channel_id=1, source_target_pairs={{0,16},{16,0},{1,17},{17,1},{2,18},{18,2},{3,19},{19,3},{4,20},{20... | collective-permute-start | bytes 3145736 | tf_op jit(solution)/shard_map/ppermute | solution.py:24
  12.8 2.4 all_to_all.33
  15.1 6.5 %all-to-all-start = ((f32[32,1,3072]{2,1,0:T(1,128)}), f32[32,1,3072]{2,1,0:T(1,128)}, u32[]{:S(2)}, u32[]{:S(2)}) async-start(f32[32,1,3072]{2,1,0:T(1,128)} %all_to_all.33), calls=%async_computation | async-start | bytes 786432 | tf_op jit(solution)/shard_map/all_to_all | solution.py:54
  22.0 1.3 copy.78
  23.4 45.9 %all-to-all-done = f32[32,1,3072]{2,1,0:T(1,128)} async-done(((f32[32,1,3072]{2,1,0:T(1,128)}), f32[32,1,3072]{2,1,0:T(1,128)}, u32[]{:S(2)}, u32[]{:S(2)}) %all-to-all-start) | async-done | bytes 393248 | tf_op jit(solution)/shard_map/all_to_all | solution.py:54
  69.2 6.7 %all-to-all-start.1 = ((f32[32,64,128]{2,1,0:T(8,128)}), f32[32,64,128]{2,1,0:T(8,128)}, u32[]{:S(2)}, u32[]{:S(2)}) async-start(f32[32,64,128]{2,1,0:T(8,128)} %bitcast.14), calls=%async_computation.1 | async-start | bytes 2097152 | tf_op jit(solution)/shard_map/all_to_all | solution.py:54
  76.5 2.4 collective-permute-done.1
  80.2 1.3 copy.79
  81.5 18.5 %all-to-all-done.1 = f32[32,64,128]{2,1,0:T(8,128)} async-done(((f32[32,64,128]{2,1,0:T(8,128)}), f32[32,64,128]{2,1,0:T(8,128)}, u32[]{:S(2)}, u32[]{:S(2)}) %all-to-all-start.1) | async-done | bytes 1048608 | tf_op jit(solution)/shard_map/all_to_all | solution.py:54
  100.0 10.0 %all-to-all-start.2 = ((f32[32,64,128]{2,1,0:T(8,128)}), f32[32,64,128]{2,1,0:T(8,128)S(1)}, u32[]{:S(2)}, u32[]{:S(2)}) async-start(f32[32,64,128]{2,1,0:T(8,128)} %bitcast.137), calls=%async_computation.2 | async-start | bytes 2097152 | tf_op jit(solution)/shard_map/all_to_all | solution.py:54
  110.0 1.1 copy.132
  112.5 1.2 reshape.191
  113.7 1.6 reshape.185
  116.2 4.5 %convolution_bitcast_fusion = f32[2048,256]{0,1:T(8,128)} fusion(f32[256,128]{1,0:T(8,128)} %reshape.185, f32[2048,128]{1,0:T(8,128)} %bitcast.15), kind=kOutput, calls=%fused_computation | convolution fusion | flops 805306368 | bytes 3276800 | tf_op jit(solution)/shard_map/dot_general | solution.py:109
  120.7 13.7 %all-to-all-done.2 = f32[32,64,128]{2,1,0:T(8,128)S(1)} async-done(((f32[32,64,128]{2,1,0:T(8,128)}), f32[32,64,128]{2,1,0:T(8,128)S(1)}, u32[]{:S(2)}, u32[]{:S(2)}) %all-to-all-start.2) | async-done | bytes 1048608 | tf_op jit(solution)/shard_map/all_to_all | solution.py:54
  134.3 1.8 fusion.16
  136.2 2.5 add_multiply_fusion
  138.8 3.6 %fusion.11 = f32[2048,128]{1,0:T(8,128)S(1)} fusion(f32[2048,256]{0,1:T(8,128)S(1)} %get-tuple-element.25, f32[128,1,256]{2,1,0:T(1,128)S(1)} %copy-done.17), kind=kOutput, calls=%fused_computation.44 | convolution fusion | flops 805306368 | bytes 3276800 | tf_op jit(solution)/shard_map/dot_general | solution.py:112
  142.4 4.8 %convolution_add_fusion = f32[2048,128]{1,0:T(8,128)} fusion(f32[2048,128]{1,0:T(8,128)S(1)} %fusion.11, f32[2048,256]{0,1:T(8,128)S(1)} %copy-done.13, f32[128,1,256]{2,1,0:T(1,128)S(1)} %copy-done.16, f32[2048,256]{0,1:T(8,128)S(1)} %get-tuple-element.26), kind=kOutput, calls=%fused_computation.2 | convolution fusion | flops 808189952 | bytes 6422528 | tf_op jit(solution)/shard_map/dot_general | solution.py:112
  147.3 9.6 %all-to-all-start.3 = ((f32[32,64,128]{2,1,0:T(8,128)}), f32[32,64,128]{2,1,0:T(8,128)}, u32[]{:S(2)}, u32[]{:S(2)}) async-start(f32[32,64,128]{2,1,0:T(8,128)} %bitcast.145), calls=%async_computation.3 | async-start | bytes 2097152 | tf_op jit(solution)/shard_map/all_to_all | solution.py:54
  156.8 4.7 %fusion.2 = f32[256,128]{1,0:T(8,128)S(1)} fusion(f32[2048,128]{1,0:T(8,128)} %bitcast.15, f32[2048,256]{0,1:T(8,128)} %copy-done.15, f32[2048,256]{0,1:T(8,128)} %copy-done.24), kind=kOutput, calls=%fused_computation.7 | convolution fusion | flops 807927808 | bytes 5373952 | tf_op jit(solution)/shard_map/dot_general | solution.py:118
  161.5 3.6 %convolution_bitcast_fusion.5 = f32[128,1,256]{2,0,1:T(8,128)S(1)} fusion(f32[2048,128]{1,0:T(8,128)S(1)} %bitcast.133, f32[2048,256]{0,1:T(8,128)} %copy-done.5), kind=kOutput, calls=%fused_computation.13 | convolution fusion | flops 805306368 | bytes 3276800 | tf_op jit(solution)/shard_map/dot_general | solution.py:115
  165.1 4.1 %convolution_bitcast_fusion.4 = f32[128,1,256]{2,0,1:T(8,128)S(1)} fusion(f32[2048,128]{1,0:T(8,128)S(1)} %bitcast.134, f32[2048,256]{0,1:T(8,128)S(1)} %copy-done.14, f32[2048,256]{0,1:T(8,128)} %copy-done.24), kind=kOutput, calls=%fused_computation.12 | convolution fusion | flops 807927808 | bytes 5373952 | tf_op jit(solution)/shard_map/dot_general | solution.py:116
  169.7 1.2 copy.88
  170.9 10.0 %all-to-all-done.3 = f32[32,64,128]{2,1,0:T(8,128)} async-done(((f32[32,64,128]{2,1,0:T(8,128)}), f32[32,64,128]{2,1,0:T(8,128)}, u32[]{:S(2)}, u32[]{:S(2)}) %all-to-all-start.3) | async-done | bytes 1048608 | tf_op jit(solution)/shard_map/all_to_all | solution.py:54
  180.9 10.3 %all-to-all-start.4 = ((f32[32,1,3072]{2,1,0:T(1,128)}), f32[32,1,3072]{2,1,0:T(1,128)}, u32[]{:S(2)}, u32[]{:S(2)}) async-start(f32[32,1,3072]{2,1,0:T(1,128)} %copy.88), calls=%async_computation.4 | async-start | bytes 786432 | tf_op jit(solution)/shard_map/all_to_all | solution.py:54
  191.3 2.0 copy.84
  194.9 1.1 broadcast_multiply_fusion
  196.1 10.5 %all-to-all-done.4 = f32[32,1,3072]{2,1,0:T(1,128)} async-done(((f32[32,1,3072]{2,1,0:T(1,128)}), f32[32,1,3072]{2,1,0:T(1,128)}, u32[]{:S(2)}, u32[]{:S(2)}) %all-to-all-start.4) | async-done | bytes 393248 | tf_op jit(solution)/shard_map/all_to_all | solution.py:54
  206.6 1.9 reduce.1
  209.6 1.7 collective-permute-start.4
  211.3 2.2 multiply_reduce_fusion.3
  213.7 1.3 collective-permute-start.3
  215.0 1.5 collective-permute-done.4
  216.5 1.3 collective-permute-start.5
  218.1 39.4 %collective-permute-done.3 = f32[128,2048]{1,0:T(8,128)S(1)} collective-permute-done((f32[128,2048]{1,0:T(8,128)S(1)}, f32[128,2048]{1,0:T(8,128)S(1)}, u32[]{:S(2)}, u32[]{:S(2)}) %collective-permute-start.3) | collective-permute-done | bytes 1048608 | tf_op jit(solution)/shard_map/ppermute | solution.py:24
  259.5 12.6 %all-to-all-start.5 = ((f32[32,1,1088]{2,1,0:T(1,128)}), f32[32,1,1088]{2,1,0:T(1,128)S(1)}, u32[]{:S(2)}, u32[]{:S(2)}) async-start(f32[32,1,1088]{2,1,0:T(1,128)} %all_to_all.41), calls=%async_computation.5 | async-start | bytes 294912 | tf_op jit(solution)/shard_map/all_to_all | solution.py:54
  272.1 1.6 add.95
  273.7 2.7 collective-permute-start.6
  276.5 6.5 %all-to-all-done.5 = f32[32,1,1088]{2,1,0:T(1,128)S(1)} async-done(((f32[32,1,1088]{2,1,0:T(1,128)}), f32[32,1,1088]{2,1,0:T(1,128)S(1)}, u32[]{:S(2)}, u32[]{:S(2)}) %all-to-all-start.5) | async-done | bytes 139296 | tf_op jit(solution)/shard_map/all_to_all | solution.py:54
  283.8 1.8 collective-permute-done.7
  285.6 1.2 collective-permute-start.8
  288.2 2.7 collective-permute-start.9
  292.9 7.2 %all-to-all-start.6 = ((f32[32,1,1088]{2,1,0:T(1,128)}), f32[32,1,1088]{2,1,0:T(1,128)S(1)}, u32[]{:S(2)}, u32[]{:S(2)}) async-start(f32[32,1,1088]{2,1,0:T(1,128)} %broadcast_in_dim.8), calls=%async_computation.6 | async-start | bytes 294912 | tf_op jit(solution)/shard_map/all_to_all | solution.py:54
  300.7 1.6 mul.271
  302.3 2.8 fusion.1
  305.2 6.2 %all-to-all-done.6 = f32[32,1,1088]{2,1,0:T(1,128)S(1)} async-done(((f32[32,1,1088]{2,1,0:T(1,128)}), f32[32,1,1088]{2,1,0:T(1,128)S(1)}, u32[]{:S(2)}, u32[]{:S(2)}) %all-to-all-start.6) | async-done | bytes 139296 | tf_op jit(solution)/shard_map/all_to_all | solution.py:54
  (122 shorter events, 19.8 us)
Async XLA Ops:
  0.6 0.8 copy-start
  0.6 11.0 %copy-start.21 = (f32[8,16,128]{2,1,0:T(8,128)S(1)}, f32[8,16,128]{2,1,0:T(8,128)}, u32[]{:S(2)}) copy-start(f32[8,16,128]{2,1,0:T(8,128)} %param.15) | copy-start | bytes 196612
  0.7 11.0 %copy-start.19 = (f32[4,2,16,256]{3,2,1,0:T(8,128)S(1)}, f32[4,2,16,256]{3,2,1,0:T(8,128)}, u32[]{:S(2)}) copy-start(f32[4,2,16,256]{3,2,1,0:T(8,128)} %param.14) | copy-start | bytes 393220
  3.8 72.2 %copy-start.2 = (f32[128,2048]{1,0:T(8,128)}, f32[128,2048]{1,0:T(8,128)S(1)}, u32[]{:S(2)}) copy-start(f32[128,2048]{1,0:T(8,128)S(1)} %convolution_bitcast_fusion.2) | copy-start | bytes 3145732
  3.8 17.9 %copy-start.11 = (f32[1,128,2048]{2,1,0:T(8,128)S(1)}, f32[1,128,2048]{2,1,0:T(8,128)}, u32[]{:S(2)}) copy-start(f32[1,128,2048]{2,1,0:T(8,128)} %param.9) | copy-start | bytes 3145732
  3.8 72.1 %collective-permute-start = (f32[128,2048]{1,0:T(8,128)S(1)}, f32[128,2048]{1,0:T(8,128)S(1)}, u32[]{:S(2)}, u32[]{:S(2)}) collective-permute-start(f32[128,2048]{1,0:T(8,128)S(1)} %convolution_bitcast_fusion.2), channel_id=1, source_target_pairs={{0,16},{16,0},{1,17},{17,1},{2,18},{18,2},{3,19},{19,3},{4,20},{20... | collective-permute-start | bytes 3145736 | tf_op jit(solution)/shard_map/ppermute | solution.py:24
  15.1 54.1 %all-to-all-start = ((f32[32,1,3072]{2,1,0:T(1,128)}), f32[32,1,3072]{2,1,0:T(1,128)}, u32[]{:S(2)}, u32[]{:S(2)}) async-start(f32[32,1,3072]{2,1,0:T(1,128)} %all_to_all.33), calls=%async_computation | async-start | bytes 786432 | tf_op jit(solution)/shard_map/all_to_all | solution.py:54
  21.9 1.4 copy-start.22
  21.9 1.4 copy-start.23
  23.4 234.1 %copy-start.18 = (f32[1,1,2048]{2,1,0:T(1,128)}, f32[1,1,2048]{2,1,0:T(1,128)S(1)}, u32[]{:S(2)}) copy-start(f32[1,1,2048]{2,1,0:T(1,128)S(1)} %get-tuple-element.28) | copy-start | bytes 24580
  69.2 30.8 %all-to-all-start.1 = ((f32[32,64,128]{2,1,0:T(8,128)}), f32[32,64,128]{2,1,0:T(8,128)}, u32[]{:S(2)}, u32[]{:S(2)}) async-start(f32[32,64,128]{2,1,0:T(8,128)} %bitcast.14), calls=%async_computation.1 | async-start | bytes 2097152 | tf_op jit(solution)/shard_map/all_to_all | solution.py:54
  75.9 3.0 copy-start.1
  75.9 2.9 copy-start.6
  76.1 3.2 %copy-start.3 = (f32[128,2048]{1,0:T(8,128)}, f32[128,2048]{1,0:T(8,128)S(1)}, u32[]{:S(2)}) copy-start(f32[128,2048]{1,0:T(8,128)S(1)} %multiply_add_fusion.2) | copy-start | bytes 3145732
  76.1 2.7 collective-permute-start.1
  78.9 1.0 copy-start.9
  78.9 1.0 copy-start.20
  100.0 34.3 %all-to-all-start.2 = ((f32[32,64,128]{2,1,0:T(8,128)}), f32[32,64,128]{2,1,0:T(8,128)S(1)}, u32[]{:S(2)}, u32[]{:S(2)}) async-start(f32[32,64,128]{2,1,0:T(8,128)} %bitcast.137), calls=%async_computation.2 | async-start | bytes 2097152 | tf_op jit(solution)/shard_map/all_to_all | solution.py:54
  116.2 18.2 %copy-start.16 = (f32[128,1,256]{2,1,0:T(1,128)S(1)}, f32[128,1,256]{2,1,0:T(1,128)}, u32[]{:S(2)}) copy-start(f32[128,1,256]{2,1,0:T(1,128)} %get-tuple-element.17) | copy-start | bytes 393220
  120.6 15.5 %copy-start.17 = (f32[128,1,256]{2,1,0:T(1,128)S(1)}, f32[128,1,256]{2,1,0:T(1,128)}, u32[]{:S(2)}) copy-start(f32[128,1,256]{2,1,0:T(1,128)} %get-tuple-element.18) | copy-start | bytes 393220
  134.3 1.9 copy-start.13
  136.2 2.6 copy-start.15
  138.8 8.5 %copy-start.5 = (f32[2048,256]{0,1:T(8,128)}, f32[2048,256]{0,1:T(8,128)S(1)}, u32[]{:S(2)}) copy-start(f32[2048,256]{0,1:T(8,128)S(1)} %get-tuple-element.25) | copy-start | bytes 6291460
  138.8 8.5 %copy-start.24 = (f32[2048,256]{0,1:T(8,128)}, f32[2048,256]{0,1:T(8,128)S(1)}, u32[]{:S(2)}) copy-start(f32[2048,256]{0,1:T(8,128)S(1)} %get-tuple-element.26) | copy-start | bytes 6291460
  147.3 33.7 %all-to-all-start.3 = ((f32[32,64,128]{2,1,0:T(8,128)}), f32[32,64,128]{2,1,0:T(8,128)}, u32[]{:S(2)}, u32[]{:S(2)}) async-start(f32[32,64,128]{2,1,0:T(8,128)} %bitcast.145), calls=%async_computation.3 | async-start | bytes 2097152 | tf_op jit(solution)/shard_map/all_to_all | solution.py:54
  161.5 3.6 %copy-start.14 = (f32[2048,256]{0,1:T(8,128)S(1)}, f32[2048,256]{0,1:T(8,128)}, u32[]{:S(2)}) copy-start(f32[2048,256]{0,1:T(8,128)} %convolution_bitcast_fusion) | copy-start | bytes 6291460
  180.9 25.7 %all-to-all-start.4 = ((f32[32,1,3072]{2,1,0:T(1,128)}), f32[32,1,3072]{2,1,0:T(1,128)}, u32[]{:S(2)}, u32[]{:S(2)}) async-start(f32[32,1,3072]{2,1,0:T(1,128)} %copy.88), calls=%async_computation.4 | async-start | bytes 786432 | tf_op jit(solution)/shard_map/all_to_all | solution.py:54
  191.3 2.7 copy-start.4
  191.3 2.7 copy-start.10
  191.3 2.7 copy-start.12
  196.0 15.3 %collective-permute-start.2 = (f32[128,2048]{1,0:T(8,128)}, f32[128,2048]{1,0:T(8,128)}, u32[]{:S(2)}, u32[]{:S(2)}) collective-permute-start(f32[128,2048]{1,0:T(8,128)} %broadcast_multiply_fusion), channel_id=1, source_target_pairs={{0,1},{1,0},{2,3},{3,2},{4,5},{5,4},{6,7},{7,6},{8,9},{9,8},{10,11... | collective-permute-start | bytes 3145736 | tf_op jit(solution)/shard_map/ppermute | solution.py:24
  209.6 6.9 %collective-permute-start.4 = (f32[49152]{0:T(1024)S(1)}, f32[49152]{0:T(1024)S(1)}, u32[]{:S(2)}, u32[]{:S(2)}) collective-permute-start(f32[49152]{0:T(1024)S(1)} %pad_maximum_fusion.2), channel_id=1, source_target_pairs={{0,32},{32,0},{64,96},{96,64},{128,160},{160,128},{192,224},{224,1... | collective-permute-start | bytes 589832 | tf_op jit(solution)/shard_map/ppermute | solution.py:24
  213.7 43.8 %collective-permute-start.3 = (f32[128,2048]{1,0:T(8,128)S(1)}, f32[128,2048]{1,0:T(8,128)S(1)}, u32[]{:S(2)}, u32[]{:S(2)}) collective-permute-start(f32[128,2048]{1,0:T(8,128)S(1)} %broadcast_multiply_fusion.1), channel_id=1, source_target_pairs={{0,16},{16,0},{1,17},{17,1},{2,18},{18,2},{3,19},{19,3},{4,20},{20... | collective-permute-start | bytes 3145736 | tf_op jit(solution)/shard_map/ppermute | solution.py:24
  216.5 55.5 %collective-permute-start.5 = (f32[49152]{0:T(1024)S(1)}, f32[49152]{0:T(1024)}, u32[]{:S(2)}, u32[]{:S(2)}) collective-permute-start(f32[49152]{0:T(1024)S(1)} %fusion.22), channel_id=1, source_target_pairs={{0,64},{64,0},{32,96},{96,32},{128,192},{192,128},{160,224},{224,1... | collective-permute-start | bytes 589832 | tf_op jit(solution)/shard_map/ppermute | solution.py:24
  257.5 1.1 copy-start.7
  258.6 43.7 %copy-start.8 = (f32[128,2048]{1,0:T(8,128)S(1)}, f32[128,2048]{1,0:T(8,128)}, u32[]{:S(2)}) copy-start(f32[128,2048]{1,0:T(8,128)} %copy-done.7) | copy-start | bytes 3145732
  259.5 23.5 %all-to-all-start.5 = ((f32[32,1,1088]{2,1,0:T(1,128)}), f32[32,1,1088]{2,1,0:T(1,128)S(1)}, u32[]{:S(2)}, u32[]{:S(2)}) async-start(f32[32,1,1088]{2,1,0:T(1,128)} %all_to_all.41), calls=%async_computation.5 | async-start | bytes 294912 | tf_op jit(solution)/shard_map/all_to_all | solution.py:54
  273.7 13.1 %collective-permute-start.6 = (f32[49152]{0:T(1024)}, f32[49152]{0:T(1024)}, u32[]{:S(2)}, u32[]{:S(2)}) collective-permute-start(f32[49152]{0:T(1024)} %add.95), channel_id=1, source_target_pairs={{0,128},{128,0},{32,160},{160,32},{64,192},{192,64},{96,224},{224,... | collective-permute-start | bytes 589832 | tf_op jit(solution)/shard_map/ppermute | solution.py:24
  283.1 2.6 collective-permute-start.7
  285.6 2.5 collective-permute-start.8
  288.2 4.1 %collective-permute-start.9 = (f32[1088]{0:T(1024)S(1)}, f32[1088]{0:T(1024)S(1)}, u32[]{:S(2)}, u32[]{:S(2)}) collective-permute-start(f32[1088]{0:T(1024)S(1)} %add.98), channel_id=1, source_target_pairs={{0,128},{128,0},{32,160},{160,32},{64,192},{192,64},{96,224},{224,... | collective-permute-start | bytes 13064 | tf_op jit(solution)/shard_map/ppermute | solution.py:24
  292.9 18.4 %all-to-all-start.6 = ((f32[32,1,1088]{2,1,0:T(1,128)}), f32[32,1,1088]{2,1,0:T(1,128)S(1)}, u32[]{:S(2)}, u32[]{:S(2)}) async-start(f32[32,1,1088]{2,1,0:T(1,128)} %broadcast_in_dim.8), calls=%async_computation.6 | async-start | bytes 294912 | tf_op jit(solution)/shard_map/all_to_all | solution.py:54
